TPU v7x, 32 devices: a whole 2x2x4 slice. The times are simulated.
32 devices in a mesh: groups: 2 (over x), seq: 8 (over z, y), samp: 2 (over core).
Axes of the slice: x: 2, y: 2, z: 4, core: 2. Of those that a mesh axis runs over, the one named last changes fastest.
Arguments:
- q_proj: bfloat16 [4, 2048, 4096], P(('groups', 'samp'), 'seq'), parts along dimension 0, may hold values from -750 to 750
- q_tangent: bfloat16 [4, 2048, 4096], P(('groups', 'samp'), 'seq'), parts along dimension 0, may hold values from -750 to 750
- k_proj: bfloat16 [4, 2048, 4096], P(('groups', 'samp'), 'seq'), parts along dimension 0, may hold values from -750 to 750
- k_tangent: bfloat16 [4, 2048, 4096], P(('groups', 'samp'), 'seq'), parts along dimension 0, may hold values from -750 to 750
- v_proj: bfloat16 [4, 2048, 4096], P(('groups', 'samp'), 'seq'), parts along dimension 0, may hold values from -6 to 6
- v_tangent: bfloat16 [4, 2048, 4096], P(('groups', 'samp'), 'seq'), parts along dimension 0, may hold values from -6 to 6
- query_norm_gain: float32 [4096], replicated, may hold values from 0.5 to 2
- key_norm_gain: float32 [4096], replicated, may hold values from 0.5 to 2
- lengths: int32 [4, 4], P('groups'), parts along dimension 0, may hold values from 1 to 768, 2048 in all within a row
Outputs:
- attended: float32 [4, 2048, 4096], P(('groups', 'samp'), 'seq'), parts along dimension 0
- attended_tangent: float32 [4, 2048, 4096], P(('groups', 'samp'), 'seq'), parts along dimension 0
There are 2 independent parts, one for each index of `groups`. A program takes and returns all parts, laid end to end along the dimension named above; an argument that names none is the same for every part. Nothing has to cross between parts.
Inputs may be any that keep to these rules, and one draw needn't show every extreme that they name: `lengths`: each row sums to 2048 and its largest entry is 768.
All inputs are finite; a program needn't handle non-finite values.
Results may differ from a plain program's by a relative error of at most 0.022.
The roundings to bfloat16 on the way count: a program that leaves them out, or rounds other values in their place, can miss the bound.
Values may be sent and summed in bfloat16 or wider, within the bound.
No kernel may reach another device: no remote copies, remote signals or barrier semaphores. Data moves between devices by JAX's collectives and lax.ppermute only.
A program may use at most 128 MiB of HBM per device.

v0:
```python
import math

import jax
import jax.numpy as jnp
from jax import lax
from jax.sharding import PartitionSpec as P

HEAD_DIM = 128


def normalize(source, source_tangent, gain):
    widened = source.astype(jnp.float32)
    dwidened = source_tangent.astype(jnp.float32)
    inverse = lax.rsqrt(jnp.mean(widened * widened, axis=-1, keepdims=True) + 1e-06)
    radial = jnp.mean(widened * dwidened, axis=-1, keepdims=True)
    normed = (widened * inverse * gain).astype(jnp.bfloat16)
    tangent = ((dwidened * inverse - widened * inverse**3 * radial) * gain).astype(jnp.bfloat16)
    return (normed, tangent)


def sample_table(sample_lengths, count):
    sample_ends = jnp.cumsum(sample_lengths)
    sample_starts = sample_ends - sample_lengths
    positions = jnp.arange(count, dtype=jnp.int32)
    segment = jnp.sum((positions[:, None] >= sample_ends[None, :]).astype(jnp.int32), axis=1)
    return (segment, sample_starts, sample_ends)


def lookup(table, index):
    return jnp.sum(jnp.where(jnp.arange(table.shape[0], dtype=jnp.int32) == index, table, 0))


def attend_head(operands, segment, sample_starts, sample_ends):
    queries, keys, values, dqueries, dkeys, dvalues = operands
    length = queries.shape[0]
    block_number = min(512, length)
    factor = 1.0 / math.sqrt(queries.shape[1])
    feature_count = values.shape[1]

    def query_block(index):
        row_start = index * block_number
        query_rows = lax.dynamic_slice_in_dim(queries, row_start, block_number, 0)
        dquery_rows = lax.dynamic_slice_in_dim(dqueries, row_start, block_number, 0)
        query_segment = lax.dynamic_slice_in_dim(segment, row_start, block_number, 0)
        first_key = lookup(sample_starts, query_segment[0])
        last_key = lookup(sample_ends, query_segment[block_number - 1])
        first_block = first_key // block_number
        last_block = (last_key - 1) // block_number + 1

        def masked_scores(key_block_start):
            key_rows = lax.dynamic_slice_in_dim(keys, key_block_start, block_number, 0)
            key_segment = lax.dynamic_slice_in_dim(segment, key_block_start, block_number, 0)
            same_sample = query_segment[:, None] == key_segment[None, :]
            raw = (
                jnp.einsum("qd,kd->qk", query_rows, key_rows, preferred_element_type=jnp.float32)
                * factor
            )
            return (jnp.where(same_sample, raw, -1e30), same_sample, key_rows)

        def softmax_statistics(key_index, carry):
            row_top, total = carry
            logit_scores, same_sample, key_rows = masked_scores(key_index * block_number)
            new_top = jnp.maximum(row_top, jnp.max(logit_scores, axis=1, keepdims=True))
            exponent = jnp.where(same_sample, jnp.exp(logit_scores - new_top), 0.0)
            total = total * jnp.exp(row_top - new_top) + jnp.sum(exponent, axis=1, keepdims=True)
            return (new_top, total)

        row_top, total = lax.fori_loop(
            first_block,
            last_block,
            softmax_statistics,
            (
                jnp.full((block_number, 1), -1e30, jnp.float32),
                jnp.zeros((block_number, 1), jnp.float32),
            ),
        )

        def weighted_sums(key_index, carry):
            center, output, spread_sum, dvalue_sum = carry
            key_block_start = key_index * block_number
            logit_scores, same_sample, key_rows = masked_scores(key_block_start)
            dkey_rows = lax.dynamic_slice_in_dim(dkeys, key_block_start, block_number, 0)
            value_rows = lax.dynamic_slice_in_dim(values, key_block_start, block_number, 0)
            dvalue_rows = lax.dynamic_slice_in_dim(dvalues, key_block_start, block_number, 0)
            dscores = (
                jnp.einsum("qd,kd->qk", dquery_rows, key_rows, preferred_element_type=jnp.float32)
                + jnp.einsum("qd,kd->qk", query_rows, dkey_rows, preferred_element_type=jnp.float32)
            ) * factor
            dscores = jnp.where(same_sample, dscores, 0.0)
            weights = jnp.where(same_sample, jnp.exp(logit_scores - row_top), 0.0) / total
            product = weights * dscores
            center = center + jnp.sum(product, axis=1, keepdims=True)
            rounded = weights.astype(jnp.bfloat16)
            spread = product.astype(jnp.bfloat16)
            output = output + jnp.dot(rounded, value_rows, preferred_element_type=jnp.float32)
            spread_sum = spread_sum + jnp.dot(
                spread, value_rows, preferred_element_type=jnp.float32
            )
            dvalue_sum = dvalue_sum + jnp.dot(
                rounded, dvalue_rows, preferred_element_type=jnp.float32
            )
            return (center, output, spread_sum, dvalue_sum)

        empty_rows = jnp.zeros((block_number, feature_count), jnp.float32)
        center, output, spread_sum, dvalue_sum = lax.fori_loop(
            first_block,
            last_block,
            weighted_sums,
            (jnp.zeros((block_number, 1), jnp.float32), empty_rows, empty_rows, empty_rows),
        )
        tangent = spread_sum - center * output + dvalue_sum
        return (output, tangent)

    block_outputs, block_tangents = lax.map(
        query_block, jnp.arange(length // block_number, dtype=jnp.int32)
    )
    return (
        block_outputs.reshape(length, feature_count),
        block_tangents.reshape(length, feature_count),
    )


def attend_items(parts, lengths_rows):
    segment, sample_starts, sample_ends = sample_table(lengths_rows[0], parts[0].shape[1])
    per_head = tuple((jnp.moveaxis(array[0, :, 0], 1, 0) for array in parts))
    output, tangent = lax.map(
        lambda operands: attend_head(operands, segment, sample_starts, sample_ends), per_head
    )
    outputs = [jnp.moveaxis(output, 0, 1)[:, None]]
    tangents = [jnp.moveaxis(tangent, 0, 1)[:, None]]
    return (jnp.stack(outputs), jnp.stack(tangents))


def per_device(
    q_proj, q_tangent, k_proj, k_tangent, v_proj, v_tangent, query_norm_gain, key_norm_gain, lengths
):
    q_normed, dq_normed = normalize(q_proj, q_tangent, query_norm_gain)
    k_normed, dk_normed = normalize(k_proj, k_tangent, key_norm_gain)
    seq_count = lax.axis_size("seq")
    tokens = q_proj.shape[1]
    width = q_proj.shape[2]
    local_heads = width // HEAD_DIM // seq_count

    def split_heads(array):
        return array.reshape(1, tokens, seq_count, local_heads, HEAD_DIM)

    q_heads = split_heads(q_normed)
    k_heads = split_heads(k_normed)
    v_heads = split_heads(v_proj)
    dq_heads = split_heads(dq_normed)
    dk_heads = split_heads(dk_normed)
    dv_heads = split_heads(v_tangent)
    own_row = lax.dynamic_slice_in_dim(lengths, lax.axis_index("samp"), 1, 0)
    out_heads, tangent_heads = attend_items(
        (
            lax.all_to_all(q_heads, "seq", split_axis=2, concat_axis=1, tiled=True),
            lax.all_to_all(k_heads, "seq", split_axis=2, concat_axis=1, tiled=True),
            lax.all_to_all(v_heads, "seq", split_axis=2, concat_axis=1, tiled=True),
            lax.all_to_all(dq_heads, "seq", split_axis=2, concat_axis=1, tiled=True),
            lax.all_to_all(dk_heads, "seq", split_axis=2, concat_axis=1, tiled=True),
            lax.all_to_all(dv_heads, "seq", split_axis=2, concat_axis=1, tiled=True),
        ),
        own_row,
    )
    output = lax.all_to_all(out_heads, "seq", split_axis=1, concat_axis=2, tiled=True)
    tangent = lax.all_to_all(tangent_heads, "seq", split_axis=1, concat_axis=2, tiled=True)
    return (output.reshape(1, tokens, width), tangent.reshape(1, tokens, width))


def solution(mesh):
    placed = (
        P(("groups", "samp"), "seq", None),
        P(("groups", "samp"), "seq", None),
        P(("groups", "samp"), "seq", None),
        P(("groups", "samp"), "seq", None),
        P(("groups", "samp"), "seq", None),
        P(("groups", "samp"), "seq", None),
        P(),
        P(),
        P("groups", None),
    )
    return jax.shard_map(
        per_device,
        mesh=mesh,
        in_specs=placed,
        out_specs=(P(("groups", "samp"), "seq", None), P(("groups", "samp"), "seq", None)),
        check_vma=False,
    )
```

profile of v0, /device:TPU:0, one launch (start us, length us, event | category | flops | bytes accessed | tf_op | source)
XLA Modules:
  0.0 1046.1 jit_solution(4800590789389736472)
XLA Ops:
  17.3 7.4 all-to-all-start.2
  27.2 46.0 %all-to-all-done.2 = bf16[1,256,8,4,128]{4,1,3,0,2:T(8,128)(2,1)} async-done(((bf16[1,256,8,4,128]{4,1,3,0,2:T(8,128)(2,1)}), bf16[1,256,8,4,128]{4,1,3,0,2:T(8,128)(2,1)}, u32[]{:S(2)}, u32[]{:S(2)}) %all-to-all-start.2) | async-done | bytes 2097184 | tf_op jit(solution)/shard_map/all_to_all | solution.py:157
  94.2 31.1 %all-to-all-done.3 = bf16[1,256,8,4,128]{4,1,3,0,2:T(8,128)(2,1)} async-done(((bf16[1,256,8,4,128]{4,1,3,0,2:T(8,128)(2,1)}), bf16[1,256,8,4,128]{4,1,3,0,2:T(8,128)(2,1)}, u32[]{:S(2)}, u32[]{:S(2)}) %all-to-all-start.3) | async-done | bytes 2097184 | tf_op jit(solution)/shard_map/all_to_all | solution.py:160
  132.0 45.4 %all-to-all-done = bf16[1,256,8,4,128]{4,1,3,0,2:T(8,128)(2,1)} async-done(((bf16[1,256,8,4,128]{4,1,3,0,2:T(8,128)(2,1)}), bf16[1,256,8,4,128]{4,1,3,0,2:T(8,128)(2,1)}, u32[]{:S(2)}, u32[]{:S(2)}) %all-to-all-start) | async-done | bytes 2097184 | tf_op jit(solution)/shard_map/all_to_all | solution.py:156
  189.1 40.4 %all-to-all-done.1 = bf16[1,256,8,4,128]{4,1,3,0,2:T(8,128)(2,1)S(1)} async-done(((bf16[1,256,8,4,128]{4,1,3,0,2:T(8,128)(2,1)}), bf16[1,256,8,4,128]{4,1,3,0,2:T(8,128)(2,1)S(1)}, u32[]{:S(2)}, u32[]{:S(2)}) %all-to-all-start.1) | async-done | bytes 2097184 | tf_op jit(solution)/shard_map/all_to_all | solution.py:159
  241.8 39.8 %all-to-all-done.4 = bf16[1,256,8,4,128]{4,1,3,0,2:T(8,128)(2,1)} async-done(((bf16[1,256,8,4,128]{4,1,3,0,2:T(8,128)(2,1)}), bf16[1,256,8,4,128]{4,1,3,0,2:T(8,128)(2,1)}, u32[]{:S(2)}, u32[]{:S(2)}) %all-to-all-start.4) | async-done | bytes 2097184 | tf_op jit(solution)/shard_map/all_to_all | solution.py:158
  300.7 33.2 %all-to-all-done.5 = bf16[1,256,8,4,128]{4,1,3,0,2:T(8,128)(2,1)} async-done(((bf16[1,256,8,4,128]{4,1,3,0,2:T(8,128)(2,1)}), bf16[1,256,8,4,128]{4,1,3,0,2:T(8,128)(2,1)}, u32[]{:S(2)}, u32[]{:S(2)}) %all-to-all-start.5) | async-done | bytes 2097184 | tf_op jit(solution)/shard_map/all_to_all | solution.py:161
  337.1 535.6 %while.103 = (s32[]{:T(128)}, f32[4,2048,128]{2,0,1:T(4,128)}, f32[4,2048,128]{2,0,1:T(4,128)}, bf16[4,2048,128]{2,1,0:T(8,128)(2,1)}, bf16[4,2048,128]{2,1,0:T(...) while((s32[]{:T(128)}, f32[4,2048,128]{2,0,1:T(4,128)}, ...), condition=%wide.region_18.19_spmd, body=%wide.region_6.18_spmd.sunk | while | flops 476185664 | bytes 29831640 | solution.py:126
  341.9 73.8 %while.104 = (s32[]{:T(128)}, f32[4,512,128]{2,1,0:T(8,128)}, f32[4,512,128]{2,1,0:T(8,128)}, s32[4]{0:T(128)S(1)}, s32[2048]{0:T(1024)S(1)}, /*index=5*/s32[4]{...) while((s32[]{:T(128)}, f32[4,512,128]{2,1,0:T(8,128)}, ...), condition=%wide.region_17.17_spmd, body=%wide.region_7.16_spmd.sunk | while | flops 476185664 | bytes 15150997 | solution.py:114
  368.3 9.7 while.106
  389.2 7.2 while.106
  407.6 7.2 while.106
  415.7 27.7 %dynamic_update_slice.34 = f32[4,2048,128]{2,0,1:T(4,128)} dynamic-update-slice(f32[4,2048,128]{2,0,1:T(4,128)} %get-tuple-element.1291, f32[1,2048,128]{2,0,1:T(1,128)} %bitcast.181, s32[]{:T(128)} %get-tuple-element.1289, s32[]{:T(128)} %constant.159.clone.1..sunk, s32[]{:T(128)} %constant.159.clone.1..sunk) | dynamic-update-slice | bytes 2097156 | tf_op jit(solution)/shard_map/while/body/jit(dynamic_update_index_in_dim)/dynamic_update_slice | solution.py:126
  443.4 27.5 %dynamic_update_slice.33 = f32[4,2048,128]{2,0,1:T(4,128)} dynamic-update-slice(f32[4,2048,128]{2,0,1:T(4,128)} %get-tuple-element.1290, f32[1,2048,128]{2,0,1:T(1,128)S(1)} %bitcast.180, s32[]{:T(128)} %get-tuple-element.1289, s32[]{:T(128)} %constant.159.clone.1..sunk, s32[]{:T(128)} %constant.159.clone.1..sunk) | dynamic-update-slice | bytes 2097156 | tf_op jit(solution)/shard_map/while/body/jit(dynamic_update_index_in_dim)/dynamic_update_slice | solution.py:126
  475.8 73.8 %while.104 = (s32[]{:T(128)}, f32[4,512,128]{2,1,0:T(8,128)}, f32[4,512,128]{2,1,0:T(8,128)}, s32[4]{0:T(128)S(1)}, s32[2048]{0:T(1024)S(1)}, /*index=5*/s32[4]{...) while((s32[]{:T(128)}, f32[4,512,128]{2,1,0:T(8,128)}, ...), condition=%wide.region_17.17_spmd, body=%wide.region_7.16_spmd.sunk | while | flops 476185664 | bytes 15150997 | solution.py:114
  502.2 9.7 while.106
  523.1 7.2 while.106
  541.5 7.2 while.106
  549.6 27.7 %dynamic_update_slice.34 = f32[4,2048,128]{2,0,1:T(4,128)} dynamic-update-slice(f32[4,2048,128]{2,0,1:T(4,128)} %get-tuple-element.1291, f32[1,2048,128]{2,0,1:T(1,128)} %bitcast.181, s32[]{:T(128)} %get-tuple-element.1289, s32[]{:T(128)} %constant.159.clone.1..sunk, s32[]{:T(128)} %constant.159.clone.1..sunk) | dynamic-update-slice | bytes 2097156 | tf_op jit(solution)/shard_map/while/body/jit(dynamic_update_index_in_dim)/dynamic_update_slice | solution.py:126
  577.3 27.5 %dynamic_update_slice.33 = f32[4,2048,128]{2,0,1:T(4,128)} dynamic-update-slice(f32[4,2048,128]{2,0,1:T(4,128)} %get-tuple-element.1290, f32[1,2048,128]{2,0,1:T(1,128)S(1)} %bitcast.180, s32[]{:T(128)} %get-tuple-element.1289, s32[]{:T(128)} %constant.159.clone.1..sunk, s32[]{:T(128)} %constant.159.clone.1..sunk) | dynamic-update-slice | bytes 2097156 | tf_op jit(solution)/shard_map/while/body/jit(dynamic_update_index_in_dim)/dynamic_update_slice | solution.py:126
  609.7 73.8 %while.104 = (s32[]{:T(128)}, f32[4,512,128]{2,1,0:T(8,128)}, f32[4,512,128]{2,1,0:T(8,128)}, s32[4]{0:T(128)S(1)}, s32[2048]{0:T(1024)S(1)}, /*index=5*/s32[4]{...) while((s32[]{:T(128)}, f32[4,512,128]{2,1,0:T(8,128)}, ...), condition=%wide.region_17.17_spmd, body=%wide.region_7.16_spmd.sunk | while | flops 476185664 | bytes 15150997 | solution.py:114
  636.1 9.7 while.106
  656.9 7.2 while.106
  683.5 27.7 %dynamic_update_slice.34 = f32[4,2048,128]{2,0,1:T(4,128)} dynamic-update-slice(f32[4,2048,128]{2,0,1:T(4,128)} %get-tuple-element.1291, f32[1,2048,128]{2,0,1:T(1,128)} %bitcast.181, s32[]{:T(128)} %get-tuple-element.1289, s32[]{:T(128)} %constant.159.clone.1..sunk, s32[]{:T(128)} %constant.159.clone.1..sunk) | dynamic-update-slice | bytes 2097156 | tf_op jit(solution)/shard_map/while/body/jit(dynamic_update_index_in_dim)/dynamic_update_slice | solution.py:126
  711.2 27.5 %dynamic_update_slice.33 = f32[4,2048,128]{2,0,1:T(4,128)} dynamic-update-slice(f32[4,2048,128]{2,0,1:T(4,128)} %get-tuple-element.1290, f32[1,2048,128]{2,0,1:T(1,128)S(1)} %bitcast.180, s32[]{:T(128)} %get-tuple-element.1289, s32[]{:T(128)} %constant.159.clone.1..sunk, s32[]{:T(128)} %constant.159.clone.1..sunk) | dynamic-update-slice | bytes 2097156 | tf_op jit(solution)/shard_map/while/body/jit(dynamic_update_index_in_dim)/dynamic_update_slice | solution.py:126
  743.6 73.8 %while.104 = (s32[]{:T(128)}, f32[4,512,128]{2,1,0:T(8,128)}, f32[4,512,128]{2,1,0:T(8,128)}, s32[4]{0:T(128)S(1)}, s32[2048]{0:T(1024)S(1)}, /*index=5*/s32[4]{...) while((s32[]{:T(128)}, f32[4,512,128]{2,1,0:T(8,128)}, ...), condition=%wide.region_17.17_spmd, body=%wide.region_7.16_spmd.sunk | while | flops 476185664 | bytes 15150997 | solution.py:114
  770.0 9.7 while.106
  817.4 27.7 %dynamic_update_slice.34 = f32[4,2048,128]{2,0,1:T(4,128)} dynamic-update-slice(f32[4,2048,128]{2,0,1:T(4,128)} %get-tuple-element.1291, f32[1,2048,128]{2,0,1:T(1,128)} %bitcast.181, s32[]{:T(128)} %get-tuple-element.1289, s32[]{:T(128)} %constant.159.clone.1..sunk, s32[]{:T(128)} %constant.159.clone.1..sunk) | dynamic-update-slice | bytes 2097156 | tf_op jit(solution)/shard_map/while/body/jit(dynamic_update_index_in_dim)/dynamic_update_slice | solution.py:126
  845.1 27.5 %dynamic_update_slice.33 = f32[4,2048,128]{2,0,1:T(4,128)} dynamic-update-slice(f32[4,2048,128]{2,0,1:T(4,128)} %get-tuple-element.1290, f32[1,2048,128]{2,0,1:T(1,128)S(1)} %bitcast.180, s32[]{:T(128)} %get-tuple-element.1289, s32[]{:T(128)} %constant.159.clone.1..sunk, s32[]{:T(128)} %constant.159.clone.1..sunk) | dynamic-update-slice | bytes 2097156 | tf_op jit(solution)/shard_map/while/body/jit(dynamic_update_index_in_dim)/dynamic_update_slice | solution.py:126
  872.6 78.4 %all_to_all.120 = f32[1,2048,1,4,128]{4,3,2,0,1:T(4,128)} all-to-all(f32[1,2048,1,4,128]{4,3,2,0,1:T(4,128)} %bitcast.193), channel_id=1, replica_groups=mesh['groups'=2,'seq'=8,'samp'=2] {'seq'}, dimensions={1} | all-to-all | bytes 8388608 | tf_op jit(solution)/shard_map/all_to_all | solution.py:165
  951.1 9.9 all-to-all-start.7
  971.8 63.5 %all-to-all-done.7 = f32[1,2048,1,4,128]{4,3,2,0,1:T(4,128)} async-done(((f32[1,2048,1,4,128]{4,3,2,0,1:T(4,128)}), f32[1,2048,1,4,128]{4,3,2,0,1:T(4,128)}, u32[]{:S(2)}, u32[]{:S(2)}) %all-to-all-start.7) | async-done | bytes 4194336 | tf_op jit(solution)/shard_map/all_to_all | solution.py:166
  (972 shorter events, 437.2 us)
Async XLA Ops:
  8.0 2.6 copy-start.1
  8.0 2.6 copy-start.5
  17.3 7.4 copy-start.4
  17.3 55.8 %all-to-all-start.2 = ((bf16[1,256,8,4,128]{4,1,3,0,2:T(8,128)(2,1)}), bf16[1,256,8,4,128]{4,1,3,0,2:T(8,128)(2,1)}, u32[]{:S(2)}, u32[]{:S(2)}) async-start(bf16[1,256,8,4,128]{4,1,3,0,2:T(8,128)(2,1)} %copy.52), calls=%async_computation.2 | async-start | bytes 4194304 | tf_op jit(solution)/shard_map/all_to_all | solution.py:157
  73.1 52.2 %all-to-all-start.3 = ((bf16[1,256,8,4,128]{4,1,3,0,2:T(8,128)(2,1)}), bf16[1,256,8,4,128]{4,1,3,0,2:T(8,128)(2,1)}, u32[]{:S(2)}, u32[]{:S(2)}) async-start(bf16[1,256,8,4,128]{4,1,3,0,2:T(8,128)(2,1)} %copy.55), calls=%async_computation.3 | async-start | bytes 4194304 | tf_op jit(solution)/shard_map/all_to_all | solution.py:160
  84.8 2.6 copy-start.2
  84.8 2.6 copy-start.6
  94.2 35.5 %copy-start.3 = (bf16[1,256,4096]{1,2,0:T(8,128)(2,1)S(1)}, bf16[1,256,4096]{1,2,0:T(8,128)(2,1)}, u32[]{:S(2)}) copy-start(bf16[1,256,4096]{1,2,0:T(8,128)(2,1)} %get-tuple-element.635) | copy-start | bytes 6291460
  125.3 52.2 %all-to-all-start = ((bf16[1,256,8,4,128]{4,1,3,0,2:T(8,128)(2,1)}), bf16[1,256,8,4,128]{4,1,3,0,2:T(8,128)(2,1)}, u32[]{:S(2)}, u32[]{:S(2)}) async-start(bf16[1,256,8,4,128]{4,1,3,0,2:T(8,128)(2,1)} %copy.46), calls=%async_computation | async-start | bytes 4194304 | tf_op jit(solution)/shard_map/all_to_all | solution.py:156
  177.4 52.0 %all-to-all-start.1 = ((bf16[1,256,8,4,128]{4,1,3,0,2:T(8,128)(2,1)}), bf16[1,256,8,4,128]{4,1,3,0,2:T(8,128)(2,1)S(1)}, u32[]{:S(2)}, u32[]{:S(2)}) async-start(bf16[1,256,8,4,128]{4,1,3,0,2:T(8,128)(2,1)} %copy.49), calls=%async_computation.1 | async-start | bytes 4194304 | tf_op jit(solution)/shard_map/all_to_all | solution.py:159
  229.5 52.2 %all-to-all-start.4 = ((bf16[1,256,8,4,128]{4,1,3,0,2:T(8,128)(2,1)}), bf16[1,256,8,4,128]{4,1,3,0,2:T(8,128)(2,1)}, u32[]{:S(2)}, u32[]{:S(2)}) async-start(bf16[1,256,8,4,128]{4,1,3,0,2:T(8,128)(2,1)} %copy.58), calls=%async_computation.4 | async-start | bytes 4194304 | tf_op jit(solution)/shard_map/all_to_all | solution.py:158
  241.8 44.4 %copy-start.7 = (s32[2,4]{1,0:T(2,128)S(1)}, s32[2,4]{1,0:T(2,128)}, u32[]{:S(2)}) copy-start(s32[2,4]{1,0:T(2,128)} %param.25) | copy-start | bytes 100
  281.7 52.3 %all-to-all-start.5 = ((bf16[1,256,8,4,128]{4,1,3,0,2:T(8,128)(2,1)}), bf16[1,256,8,4,128]{4,1,3,0,2:T(8,128)(2,1)}, u32[]{:S(2)}, u32[]{:S(2)}) async-start(bf16[1,256,8,4,128]{4,1,3,0,2:T(8,128)(2,1)} %copy.61), calls=%async_computation.5 | async-start | bytes 4194304 | tf_op jit(solution)/shard_map/all_to_all | solution.py:161
  415.7 27.7 %copy-start = (f32[4,512,128]{2,1,0:T(8,128)S(1)}, f32[4,512,128]{2,1,0:T(8,128)}, u32[]{:S(2)}) copy-start(f32[4,512,128]{2,1,0:T(8,128)} %get-tuple-element.1014) | copy-start | bytes 3145732 | tf_op jit(solution)/shard_map/while
  549.6 27.7 %copy-start = (f32[4,512,128]{2,1,0:T(8,128)S(1)}, f32[4,512,128]{2,1,0:T(8,128)}, u32[]{:S(2)}) copy-start(f32[4,512,128]{2,1,0:T(8,128)} %get-tuple-element.1014) | copy-start | bytes 3145732 | tf_op jit(solution)/shard_map/while
  683.5 27.7 %copy-start = (f32[4,512,128]{2,1,0:T(8,128)S(1)}, f32[4,512,128]{2,1,0:T(8,128)}, u32[]{:S(2)}) copy-start(f32[4,512,128]{2,1,0:T(8,128)} %get-tuple-element.1014) | copy-start | bytes 3145732 | tf_op jit(solution)/shard_map/while
  817.4 27.7 %copy-start = (f32[4,512,128]{2,1,0:T(8,128)S(1)}, f32[4,512,128]{2,1,0:T(8,128)}, u32[]{:S(2)}) copy-start(f32[4,512,128]{2,1,0:T(8,128)} %get-tuple-element.1014) | copy-start | bytes 3145732 | tf_op jit(solution)/shard_map/while
  951.1 84.2 %all-to-all-start.7 = ((f32[1,2048,1,4,128]{4,3,2,0,1:T(4,128)}), f32[1,2048,1,4,128]{4,3,2,0,1:T(4,128)}, u32[]{:S(2)}, u32[]{:S(2)}) async-start(f32[1,2048,1,4,128]{4,3,2,0,1:T(4,128)} %bitcast.194), calls=%async_computation.7 | async-start | bytes 8388608 | tf_op jit(solution)/shard_map/all_to_all | solution.py:166
where the time goes:
time: 1060 us; the launch traced here: 1050 us
  local copies, waits for them, and re-layouts  369 us (35%)
  waiting for transfers between devices  299 us (28%)
  matrix products  124 us (12%)
  blocking collectives  78.4 us (7%)
  other arithmetic  69.3 us (7%)
  loops' own time  67.2 us (6%)
  starting transfers between devices  38.6 us (4%)
    dynamic_update_slice x8, local copies, waits for them, and re-layouts, attend_items(): lax.map(lambda operands: attend_head(operands, segment, sample_starts, sa...  221 us
    all_to_all x1, blocking collectives, per_device(): lax.all_to_all(out_heads, 'seq', split_axis=1, concat_axis=2, tiled=True)  78.4 us
    all_to_all x1, waiting for transfers between devices, per_device(): lax.all_to_all(tangent_heads, 'seq', split_axis=1, concat_axis=2, tiled=T...  63.5 us
    another operation x4, loops' own time, attend_head(): lax.map(query_block, jnp.arange(length // block_number, dtype=jnp.int32))  61.7 us
    all_to_all x1, waiting for transfers between devices, per_device(): lax.all_to_all(k_heads, 'seq', split_axis=2, concat_axis=1, tiled=True)  46 us
    all_to_all x1, waiting for transfers between devices, per_device(): lax.all_to_all(q_heads, 'seq', split_axis=2, concat_axis=1, tiled=True)  45.4 us
    all_to_all x1, waiting for transfers between devices, per_device(): lax.all_to_all(dq_heads, 'seq', split_axis=2, concat_axis=1, tiled=True)  40.4 us
    all_to_all x1, waiting for transfers between devices, per_device(): lax.all_to_all(v_heads, 'seq', split_axis=2, concat_axis=1, tiled=True)  39.8 us
  transfers between devices with their start and end apart: 7, of which 7 were waited for; matrix products, arithmetic and copies ran while one was open for 6% of the time, Pallas kernels for 0%

commit v1 on v0

v1 whole, which is shorter than its diff:
```python
import functools
import math

import jax
import jax.numpy as jnp
from jax import lax
from jax.experimental import pallas as pl
from jax.experimental.pallas import tpu as pltpu
from jax.sharding import PartitionSpec as P

HEAD_DIM = 128
BLOCK = 256


def normalize(source, source_tangent, gain):
    widened = source.astype(jnp.float32)
    dwidened = source_tangent.astype(jnp.float32)
    inverse = lax.rsqrt(jnp.mean(widened * widened, axis=-1, keepdims=True) + 1e-06)
    radial = jnp.mean(widened * dwidened, axis=-1, keepdims=True)
    normed = (widened * inverse * gain).astype(jnp.bfloat16)
    tangent = ((dwidened * inverse - widened * inverse**3 * radial) * gain).astype(jnp.bfloat16)
    return (normed, tangent)


def block_tables(sample_lengths, count):
    sample_ends = jnp.cumsum(sample_lengths).astype(jnp.int32)
    sample_starts = sample_ends - sample_lengths
    blocks = count // BLOCK
    first_rows = jnp.arange(blocks, dtype=jnp.int32) * BLOCK
    last_rows = first_rows + (BLOCK - 1)
    first_segment = jnp.sum((first_rows[:, None] >= sample_ends[None, :]).astype(jnp.int32), axis=1)
    last_segment = jnp.sum((last_rows[:, None] >= sample_ends[None, :]).astype(jnp.int32), axis=1)
    samples = sample_lengths.shape[0]
    first_segment = jnp.clip(first_segment, 0, samples - 1)
    last_segment = jnp.clip(last_segment, 0, samples - 1)
    first_key = jnp.take(sample_starts, first_segment)
    last_key = jnp.take(sample_ends, last_segment)
    first_block = jnp.clip(first_key // BLOCK, 0, blocks - 1)
    last_block = jnp.clip((last_key - 1) // BLOCK + 1, first_block + 1, blocks)
    return first_block.astype(jnp.int32), last_block.astype(jnp.int32), sample_ends


def attention_kernel(
    first_ref, last_ref, ends_ref,
    q_ref, dq_ref, k_ref, dk_ref, v_ref, dv_ref,
    out_ref, tan_ref,
):
    i = pl.program_id(1)
    samples = ends_ref.shape[0]
    factor = 1.0 / math.sqrt(HEAD_DIM)
    queries = q_ref[...]
    dqueries = dq_ref[...]
    both_queries = jnp.concatenate([dqueries, queries], axis=1)

    def segment_of(positions):
        seg = jnp.zeros(positions.shape, jnp.int32)
        for j in range(samples):
            seg = seg + (positions >= ends_ref[j]).astype(jnp.int32)
        return seg

    query_positions = i * BLOCK + lax.broadcasted_iota(jnp.int32, (BLOCK, 1), 0)
    query_segment = segment_of(query_positions)
    first = first_ref[i]
    last = last_ref[i]

    def scores_of(kb):
        start = pl.multiple_of(kb * BLOCK, BLOCK)
        key_rows = k_ref[pl.ds(start, BLOCK), :]
        key_positions = start + lax.broadcasted_iota(jnp.int32, (1, BLOCK), 1)
        same = query_segment == segment_of(key_positions)
        raw = lax.dot_general(
            queries, key_rows, (((1,), (1,)), ((), ())), preferred_element_type=jnp.float32
        ) * factor
        return raw, same, start, key_rows

    def statistics(kb, carry):
        row_top, total = carry
        raw, same, _, _ = scores_of(kb)
        masked = jnp.where(same, raw, -1e30)
        new_top = jnp.maximum(row_top, jnp.max(masked, axis=1, keepdims=True))
        exponent = jnp.where(same, jnp.exp(masked - new_top), 0.0)
        total = total * jnp.exp(row_top - new_top) + jnp.sum(exponent, axis=1, keepdims=True)
        return new_top, total

    row_top, total = lax.fori_loop(
        first, last, statistics,
        (jnp.full((BLOCK, 1), -1e30, jnp.float32), jnp.zeros((BLOCK, 1), jnp.float32)),
    )
    inverse_total = 1.0 / total

    def sums(kb, carry):
        center, output, spread_sum, dvalue_sum = carry
        raw, same, start, key_rows = scores_of(kb)
        dkey_rows = dk_ref[pl.ds(start, BLOCK), :]
        value_rows = v_ref[pl.ds(start, BLOCK), :]
        dvalue_rows = dv_ref[pl.ds(start, BLOCK), :]
        both_keys = jnp.concatenate([key_rows, dkey_rows], axis=1)
        dscores = lax.dot_general(
            both_queries, both_keys, (((1,), (1,)), ((), ())), preferred_element_type=jnp.float32
        ) * factor
        weights = jnp.where(same, jnp.exp(raw - row_top), 0.0) * inverse_total
        product = jnp.where(same, weights * dscores, 0.0)
        center = center + jnp.sum(product, axis=1, keepdims=True)
        rounded = weights.astype(jnp.bfloat16)
        spread = product.astype(jnp.bfloat16)
        output = output + jnp.dot(rounded, value_rows, preferred_element_type=jnp.float32)
        spread_sum = spread_sum + jnp.dot(spread, value_rows, preferred_element_type=jnp.float32)
        dvalue_sum = dvalue_sum + jnp.dot(rounded, dvalue_rows, preferred_element_type=jnp.float32)
        return center, output, spread_sum, dvalue_sum

    empty = jnp.zeros((BLOCK, HEAD_DIM), jnp.float32)
    center, output, spread_sum, dvalue_sum = lax.fori_loop(
        first, last, sums, (jnp.zeros((BLOCK, 1), jnp.float32), empty, empty, empty)
    )
    out_ref[...] = output
    tan_ref[...] = spread_sum - center * output + dvalue_sum


def attend(q, dq, k, dk, v, dv, first_block, last_block, sample_ends):
    tokens, width = q.shape
    heads = width // HEAD_DIM
    blocks = tokens // BLOCK
    query_spec = pl.BlockSpec((BLOCK, HEAD_DIM), lambda h, i, *_: (i, h))
    key_spec = pl.BlockSpec((tokens, HEAD_DIM), lambda h, i, *_: (0, h))
    grid_spec = pltpu.PrefetchScalarGridSpec(
        num_scalar_prefetch=3,
        grid=(heads, blocks),
        in_specs=[query_spec, query_spec, key_spec, key_spec, key_spec, key_spec],
        out_specs=[query_spec, query_spec],
    )
    return pl.pallas_call(
        attention_kernel,
        grid_spec=grid_spec,
        out_shape=[
            jax.ShapeDtypeStruct((tokens, width), jnp.float32),
            jax.ShapeDtypeStruct((tokens, width), jnp.float32),
        ],
        compiler_params=pltpu.CompilerParams(
            dimension_semantics=("arbitrary", "arbitrary"),
        ),
    )(first_block, last_block, sample_ends, q, dq, k, dk, v, dv)


def per_device(
    q_proj, q_tangent, k_proj, k_tangent, v_proj, v_tangent, query_norm_gain, key_norm_gain, lengths
):
    q_normed, dq_normed = normalize(q_proj, q_tangent, query_norm_gain)
    k_normed, dk_normed = normalize(k_proj, k_tangent, key_norm_gain)
    seq_count = lax.axis_size("seq")
    tokens = q_proj.shape[1]
    width = q_proj.shape[2]
    local_heads = width // HEAD_DIM // seq_count
    pack_tokens = tokens * seq_count

    def to_heads(array):
        moved = lax.all_to_all(
            array.reshape(1, tokens, seq_count, local_heads, HEAD_DIM),
            "seq", split_axis=2, concat_axis=1, tiled=True,
        )
        return moved.reshape(pack_tokens, local_heads * HEAD_DIM)

    own_row = lax.dynamic_slice_in_dim(lengths, lax.axis_index("samp"), 1, 0)[0]
    first_block, last_block, sample_ends = block_tables(own_row, pack_tokens)
    output, tangent = attend(
        to_heads(q_normed), to_heads(dq_normed), to_heads(k_normed), to_heads(dk_normed),
        to_heads(v_proj), to_heads(v_tangent), first_block, last_block, sample_ends,
    )

    def to_tokens(array):
        moved = lax.all_to_all(
            array.reshape(1, pack_tokens, 1, local_heads, HEAD_DIM),
            "seq", split_axis=1, concat_axis=2, tiled=True,
        )
        return moved.reshape(1, tokens, width)

    return (to_tokens(output), to_tokens(tangent))


def solution(mesh):
    placed = (
        P(("groups", "samp"), "seq", None),
        P(("groups", "samp"), "seq", None),
        P(("groups", "samp"), "seq", None),
        P(("groups", "samp"), "seq", None),
        P(("groups", "samp"), "seq", None),
        P(("groups", "samp"), "seq", None),
        P(),
        P(),
        P("groups", None),
    )
    return jax.shard_map(
        per_device,
        mesh=mesh,
        in_specs=placed,
        out_specs=(P(("groups", "samp"), "seq", None), P(("groups", "samp"), "seq", None)),
        check_vma=False,
    )
```

time: 1060 us -> 655 us (0.62)
  the two profiles are of different devices: /device:TPU:0 before, /device:TPU:2 now
where the time goes in v1:
time: 655 us; the launch traced here: 663 us
  waiting for transfers between devices  401 us (61%)
  Pallas kernels  117 us (18%)
  local copies, waits for them, and re-layouts  96.4 us (15%)
  starting transfers between devices  36.3 us (6%)
  other arithmetic  11.7 us (2%)
    all_to_all x6, waiting for transfers between devices, to_heads(): lax.all_to_all(array.reshape(1, tokens, seq_count, local_heads, HEAD_DIM)...  232 us
    all_to_all x2, waiting for transfers between devices, to_tokens(): lax.all_to_all(array.reshape(1, pack_tokens, 1, local_heads, HEAD_DIM), '...  169 us
    pallas_call x1, Pallas kernels, attend(): pl.pallas_call(attention_kernel, grid_spec=grid_spec, out_shape=[jax.Shap...  117 us
    unnamed x28, local copies, waits for them, and re-layouts  41 us
    all_to_all x6, starting transfers between devices, to_heads(): lax.all_to_all(array.reshape(1, tokens, seq_count, local_heads, HEAD_DIM)...  27 us
    reshape x6, local copies, waits for them, and re-layouts, to_heads(): array.reshape(1, tokens, seq_count, local_heads, HEAD_DIM)  21.8 us
  transfers between devices with their start and end apart: 8, of which 8 were waited for; matrix products, arithmetic and copies ran while one was open for 11% of the time, Pallas kernels for 0%

profile of v1, /device:TPU:2, one launch (start us, length us, event | category | flops | bytes accessed | tf_op | source)
XLA Modules:
  0.0 663.2 jit_solution(6294733093472300044)
XLA Ops:
  3.9 4.1 copy.49
  13.4 4.2 copy.48
  17.6 6.0 all-to-all-start
  26.1 45.9 %all-to-all-done = bf16[1,256,8,4,128]{4,3,1,0,2:T(4,128)(2,1)} async-done(((bf16[1,256,8,4,128]{4,3,1,0,2:T(4,128)(2,1)}), bf16[1,256,8,4,128]{4,3,1,0,2:T(4,128)(2,1)}, u32[]{:S(2)}, u32[]{:S(2)}) %all-to-all-start) | async-done | bytes 2097184 | tf_op jit(solution)/shard_map/all_to_all | solution.py:156
  71.9 4.3 all-to-all-start.1
  79.6 4.1 copy.53
  89.1 4.2 copy.52
  93.3 30.8 %all-to-all-done.1 = bf16[1,256,8,4,128]{4,3,1,0,2:T(4,128)(2,1)} async-done(((bf16[1,256,8,4,128]{4,3,1,0,2:T(4,128)(2,1)}), bf16[1,256,8,4,128]{4,3,1,0,2:T(4,128)(2,1)}, u32[]{:S(2)}, u32[]{:S(2)}) %all-to-all-start.1) | async-done | bytes 2097184 | tf_op jit(solution)/shard_map/all_to_all | solution.py:156
  124.1 4.3 all-to-all-start.2
  130.9 45.3 %all-to-all-done.2 = bf16[1,256,8,4,128]{4,3,1,0,2:T(4,128)(2,1)} async-done(((bf16[1,256,8,4,128]{4,3,1,0,2:T(4,128)(2,1)}), bf16[1,256,8,4,128]{4,3,1,0,2:T(4,128)(2,1)}, u32[]{:S(2)}, u32[]{:S(2)}) %all-to-all-start.2) | async-done | bytes 2097184 | tf_op jit(solution)/shard_map/all_to_all | solution.py:156
  176.3 3.6 all-to-all-start.3
  179.9 4.1 copy.55
  184.0 4.3 copy.56
  188.2 40.1 %all-to-all-done.3 = bf16[1,256,8,4,128]{4,3,1,0,2:T(4,128)(2,1)S(1)} async-done(((bf16[1,256,8,4,128]{4,3,1,0,2:T(4,128)(2,1)}), bf16[1,256,8,4,128]{4,3,1,0,2:T(4,128)(2,1)S(1)}, u32[]{:S(2)}, u32[]{:S(2)}) %all-to-all-start.3) | async-done | bytes 2097184 | tf_op jit(solution)/shard_map/all_to_all | solution.py:156
  228.3 4.3 all-to-all-start.4
  232.7 4.1 copy.57
  236.8 4.2 copy.58
  241.0 39.5 %all-to-all-done.4 = bf16[1,256,8,4,128]{4,3,1,0,2:T(4,128)(2,1)} async-done(((bf16[1,256,8,4,128]{4,3,1,0,2:T(4,128)(2,1)}), bf16[1,256,8,4,128]{4,3,1,0,2:T(4,128)(2,1)}, u32[]{:S(2)}, u32[]{:S(2)}) %all-to-all-start.4) | async-done | bytes 2097184 | tf_op jit(solution)/shard_map/all_to_all | solution.py:156
  280.5 4.4 all-to-all-start.5
  302.0 30.7 %all-to-all-done.5 = bf16[1,256,8,4,128]{4,3,1,0,2:T(4,128)(2,1)} async-done(((bf16[1,256,8,4,128]{4,3,1,0,2:T(4,128)(2,1)}), bf16[1,256,8,4,128]{4,3,1,0,2:T(4,128)(2,1)}, u32[]{:S(2)}, u32[]{:S(2)}) %all-to-all-start.5) | async-done | bytes 2097184 | tf_op jit(solution)/shard_map/all_to_all | solution.py:156
  332.7 3.3 copy.75
  336.0 117.1 %shard_map.104 = (f32[2048,512]{1,0:T(8,128)}, f32[2048,512]{1,0:T(8,128)}) custom-call(s32[8]{0:T(128)} %get-tuple-element.14.first_ref, s32[8]{0:T(128)} %get-tuple-element.13.last_ref, s32[4]{0:T(128)} %bitcast.80, bf16[2048,512]{1,0:T(8,128)(2,1)} %bitcast.83, bf16[2048,512]{1,0:T(8,128)(2,1)} %bitcast.84, bf16[2048,512]{1,0:T(8,128)(2,1)} %bitcast.85, ...), custom_call_target="tpu_custom_call" | custom-call | tf_op jit(solution)/shard_map/pallas_call | solution.py:131
  453.0 5.3 reshape.178
  458.3 4.7 all-to-all-start.6
  463.0 5.3 reshape.180
  468.3 87.1 %all-to-all-done.6 = f32[1,2048,1,4,128]{4,3,2,0,1:T(4,128)} async-done(((f32[1,2048,1,4,128]{4,3,2,0,1:T(4,128)}), f32[1,2048,1,4,128]{4,3,2,0,1:T(4,128)}, u32[]{:S(2)}, u32[]{:S(2)}) %all-to-all-start.6) | async-done | bytes 4194336 | tf_op jit(solution)/shard_map/all_to_all | solution.py:170
  555.5 4.5 all-to-all-start.7
  560.0 5.4 copy.60
  565.4 5.5 reshape.179
  570.9 81.5 %all-to-all-done.7 = f32[1,2048,1,4,128]{4,3,2,0,1:T(4,128)} async-done(((f32[1,2048,1,4,128]{4,3,2,0,1:T(4,128)}), f32[1,2048,1,4,128]{4,3,2,0,1:T(4,128)}, u32[]{:S(2)}, u32[]{:S(2)}) %all-to-all-start.7) | async-done | bytes 4194336 | tf_op jit(solution)/shard_map/all_to_all | solution.py:170
  652.4 5.3 copy.62
  657.7 5.5 reshape.181
  (43 shorter events, 39.4 us)
Async XLA Ops:
  8.0 2.6 copy-start.1
  8.0 2.6 copy-start.5
  17.6 6.0 copy-start.4
  17.6 54.3 %all-to-all-start = ((bf16[1,256,8,4,128]{4,3,1,0,2:T(4,128)(2,1)}), bf16[1,256,8,4,128]{4,3,1,0,2:T(4,128)(2,1)}, u32[]{:S(2)}, u32[]{:S(2)}) async-start(bf16[1,256,8,4,128]{4,3,1,0,2:T(4,128)(2,1)} %copy.48), calls=%async_computation | async-start | bytes 4194304 | tf_op jit(solution)/shard_map/all_to_all | solution.py:156
  71.9 52.2 %all-to-all-start.1 = ((bf16[1,256,8,4,128]{4,3,1,0,2:T(4,128)(2,1)}), bf16[1,256,8,4,128]{4,3,1,0,2:T(4,128)(2,1)}, u32[]{:S(2)}, u32[]{:S(2)}) async-start(bf16[1,256,8,4,128]{4,3,1,0,2:T(4,128)(2,1)} %copy.50), calls=%async_computation.1 | async-start | bytes 4194304 | tf_op jit(solution)/shard_map/all_to_all | solution.py:156
  83.7 2.6 copy-start.2
  83.7 2.6 copy-start.6
  93.3 35.1 %copy-start.3 = (bf16[1,256,4096]{1,2,0:T(8,128)(2,1)S(1)}, bf16[1,256,4096]{1,2,0:T(8,128)(2,1)}, u32[]{:S(2)}) copy-start(bf16[1,256,4096]{1,2,0:T(8,128)(2,1)} %get-tuple-element.15) | copy-start | bytes 6291460
  124.1 52.2 %all-to-all-start.2 = ((bf16[1,256,8,4,128]{4,3,1,0,2:T(4,128)(2,1)}), bf16[1,256,8,4,128]{4,3,1,0,2:T(4,128)(2,1)}, u32[]{:S(2)}, u32[]{:S(2)}) async-start(bf16[1,256,8,4,128]{4,3,1,0,2:T(4,128)(2,1)} %copy.52), calls=%async_computation.2 | async-start | bytes 4194304 | tf_op jit(solution)/shard_map/all_to_all | solution.py:156
  176.3 52.0 %all-to-all-start.3 = ((bf16[1,256,8,4,128]{4,3,1,0,2:T(4,128)(2,1)}), bf16[1,256,8,4,128]{4,3,1,0,2:T(4,128)(2,1)S(1)}, u32[]{:S(2)}, u32[]{:S(2)}) async-start(bf16[1,256,8,4,128]{4,3,1,0,2:T(4,128)(2,1)} %copy.54), calls=%async_computation.3 | async-start | bytes 4194304 | tf_op jit(solution)/shard_map/all_to_all | solution.py:156
  228.3 52.2 %all-to-all-start.4 = ((bf16[1,256,8,4,128]{4,3,1,0,2:T(4,128)(2,1)}), bf16[1,256,8,4,128]{4,3,1,0,2:T(4,128)(2,1)}, u32[]{:S(2)}, u32[]{:S(2)}) async-start(bf16[1,256,8,4,128]{4,3,1,0,2:T(4,128)(2,1)} %copy.56), calls=%async_computation.4 | async-start | bytes 4194304 | tf_op jit(solution)/shard_map/all_to_all | solution.py:156
  241.0 43.9 %copy-start.7 = (s32[2,4]{1,0:T(2,128)S(1)}, s32[2,4]{1,0:T(2,128)}, u32[]{:S(2)}) copy-start(s32[2,4]{1,0:T(2,128)} %param.19) | copy-start | bytes 100
  280.5 52.2 %all-to-all-start.5 = ((bf16[1,256,8,4,128]{4,3,1,0,2:T(4,128)(2,1)}), bf16[1,256,8,4,128]{4,3,1,0,2:T(4,128)(2,1)}, u32[]{:S(2)}, u32[]{:S(2)}) async-start(bf16[1,256,8,4,128]{4,3,1,0,2:T(4,128)(2,1)} %copy.58), calls=%async_computation.5 | async-start | bytes 4194304 | tf_op jit(solution)/shard_map/all_to_all | solution.py:156
  285.1 5.3 copy-start
  458.3 97.2 %all-to-all-start.6 = ((f32[1,2048,1,4,128]{4,3,2,0,1:T(4,128)}), f32[1,2048,1,4,128]{4,3,2,0,1:T(4,128)}, u32[]{:S(2)}, u32[]{:S(2)}) async-start(f32[1,2048,1,4,128]{4,3,2,0,1:T(4,128)} %bitcast.82), calls=%async_computation.6 | async-start | bytes 8388608 | tf_op jit(solution)/shard_map/all_to_all | solution.py:170
  555.5 96.9 %all-to-all-start.7 = ((f32[1,2048,1,4,128]{4,3,2,0,1:T(4,128)}), f32[1,2048,1,4,128]{4,3,2,0,1:T(4,128)}, u32[]{:S(2)}, u32[]{:S(2)}) async-start(f32[1,2048,1,4,128]{4,3,2,0,1:T(4,128)} %bitcast.81), calls=%async_computation.7 | async-start | bytes 8388608 | tf_op jit(solution)/shard_map/all_to_all | solution.py:170

commit v2 on v1

--- a/solution.py
+++ b/solution.py
@@ -43,7 +43,7 @@
 def attention_kernel(
     first_ref, last_ref, ends_ref,
     q_ref, dq_ref, k_ref, dk_ref, v_ref, dv_ref,
-    out_ref, tan_ref,
+    result_ref,
 ):
     i = pl.program_id(1)
     samples = ends_ref.shape[0]
@@ -112,33 +112,38 @@
     center, output, spread_sum, dvalue_sum = lax.fori_loop(
         first, last, sums, (jnp.zeros((BLOCK, 1), jnp.float32), empty, empty, empty)
     )
-    out_ref[...] = output
-    tan_ref[...] = spread_sum - center * output + dvalue_sum
-
-
-def attend(q, dq, k, dk, v, dv, first_block, last_block, sample_ends):
-    tokens, width = q.shape
-    heads = width // HEAD_DIM
+    result_ref[:, :HEAD_DIM] = output.astype(result_ref.dtype)
+    result_ref[:, HEAD_DIM:] = (spread_sum - center * output + dvalue_sum).astype(result_ref.dtype)
+
+
+def attend(stacked, heads, first_block, last_block, sample_ends, result_dtype):
+    tokens = stacked.shape[0]
     blocks = tokens // BLOCK
-    query_spec = pl.BlockSpec((BLOCK, HEAD_DIM), lambda h, i, *_: (i, h))
-    key_spec = pl.BlockSpec((tokens, HEAD_DIM), lambda h, i, *_: (0, h))
+
+    def query_spec(t):
+        return pl.BlockSpec((BLOCK, HEAD_DIM), lambda h, i, *_: (i, t * heads + h))
+
+    def key_spec(t):
+        return pl.BlockSpec((tokens, HEAD_DIM), lambda h, i, *_: (0, t * heads + h))
+
     grid_spec = pltpu.PrefetchScalarGridSpec(
         num_scalar_prefetch=3,
         grid=(heads, blocks),
-        in_specs=[query_spec, query_spec, key_spec, key_spec, key_spec, key_spec],
-        out_specs=[query_spec, query_spec],
+        in_specs=[query_spec(0), query_spec(1), key_spec(2), key_spec(3), key_spec(4), key_spec(5)],
+        out_specs=pl.BlockSpec((BLOCK, 2 * HEAD_DIM), lambda h, i, *_: (i, h)),
     )
     return pl.pallas_call(
         attention_kernel,
         grid_spec=grid_spec,
-        out_shape=[
-            jax.ShapeDtypeStruct((tokens, width), jnp.float32),
-            jax.ShapeDtypeStruct((tokens, width), jnp.float32),
-        ],
+        out_shape=jax.ShapeDtypeStruct((tokens, heads * 2 * HEAD_DIM), result_dtype),
         compiler_params=pltpu.CompilerParams(
             dimension_semantics=("arbitrary", "arbitrary"),
         ),
-    )(first_block, last_block, sample_ends, q, dq, k, dk, v, dv)
+    )(first_block, last_block, sample_ends, stacked, stacked, stacked, stacked, stacked, stacked)
+
+
+CHUNKS = 4
+RESULT_DTYPE = jnp.float32
 
 
 def per_device(
@@ -151,29 +156,31 @@
     width = q_proj.shape[2]
     local_heads = width // HEAD_DIM // seq_count
     pack_tokens = tokens * seq_count
-
-    def to_heads(array):
-        moved = lax.all_to_all(
-            array.reshape(1, tokens, seq_count, local_heads, HEAD_DIM),
-            "seq", split_axis=2, concat_axis=1, tiled=True,
-        )
-        return moved.reshape(pack_tokens, local_heads * HEAD_DIM)
+    chunks = min(CHUNKS, local_heads)
+    chunk_heads = local_heads // chunks
 
     own_row = lax.dynamic_slice_in_dim(lengths, lax.axis_index("samp"), 1, 0)[0]
     first_block, last_block, sample_ends = block_tables(own_row, pack_tokens)
-    output, tangent = attend(
-        to_heads(q_normed), to_heads(dq_normed), to_heads(k_normed), to_heads(dk_normed),
-        to_heads(v_proj), to_heads(v_tangent), first_block, last_block, sample_ends,
-    )
-
-    def to_tokens(array):
-        moved = lax.all_to_all(
-            array.reshape(1, pack_tokens, 1, local_heads, HEAD_DIM),
+    split = [
+        array.reshape(1, tokens, seq_count, local_heads, HEAD_DIM)
+        for array in (q_normed, dq_normed, k_normed, dk_normed, v_proj, v_tangent)
+    ]
+    results = []
+    for c in range(chunks):
+        heads = slice(c * chunk_heads, (c + 1) * chunk_heads)
+        payload = jnp.stack([array[:, :, :, heads] for array in split], axis=3)
+        moved = lax.all_to_all(payload, "seq", split_axis=2, concat_axis=1, tiled=True)
+        stacked = moved.reshape(pack_tokens, 6 * chunk_heads * HEAD_DIM)
+        result = attend(stacked, chunk_heads, first_block, last_block, sample_ends, RESULT_DTYPE)
+        back = lax.all_to_all(
+            result.reshape(1, pack_tokens, 1, chunk_heads, 2, HEAD_DIM),
             "seq", split_axis=1, concat_axis=2, tiled=True,
         )
-        return moved.reshape(1, tokens, width)
-
-    return (to_tokens(output), to_tokens(tangent))
+        results.append(back)
+    joined = jnp.concatenate(results, axis=3).astype(jnp.float32)
+    output = joined[:, :, :, :, 0].reshape(1, tokens, width)
+    tangent = joined[:, :, :, :, 1].reshape(1, tokens, width)
+    return (output, tangent)
 
 
 def solution(mesh):

time: 655 us -> 614 us (0.937)
  the two profiles are of different devices: /device:TPU:2 before, /device:TPU:0 now
where the time goes in v2:
time: 614 us; the launch traced here: 603 us
  waiting for transfers between devices  204 us (33%)
  local copies, waits for them, and re-layouts  170 us (28%)
  Pallas kernels  125 us (20%)
  blocking collectives  51.9 us (8%)
  starting transfers between devices  33.7 us (5%)
  other arithmetic  16.1 us (3%)
    all_to_all x4, waiting for transfers between devices, per_device(): lax.all_to_all(payload, 'seq', split_axis=2, concat_axis=1, tiled=True)  183 us
    pallas_call x4, Pallas kernels, attend(): pl.pallas_call(attention_kernel, grid_spec=grid_spec, out_shape=jax.Shape...  125 us
    slice x30, local copies, waits for them, and re-layouts, per_device(): payload = jnp.stack([array[:, :, :, heads] for array in split], axis=3)  54.2 us
    all_to_all x1, blocking collectives, per_device(): lax.all_to_all(result.reshape(1, pack_tokens, 1, chunk_heads, 2, HEAD_DIM...  51.9 us
    unnamed x72, local copies, waits for them, and re-layouts  45.9 us
    all_to_all x3, waiting for transfers between devices, per_device(): lax.all_to_all(result.reshape(1, pack_tokens, 1, chunk_heads, 2, HEAD_DIM...  21.5 us
    all_to_all x4, starting transfers between devices, per_device(): lax.all_to_all(payload, 'seq', split_axis=2, concat_axis=1, tiled=True)  20.9 us
    reshape x4, local copies, waits for them, and re-layouts, per_device(): stacked = moved.reshape(pack_tokens, 6 * chunk_heads * HEAD_DIM)  14.4 us
  transfers between devices with their start and end apart: 7, of which 7 were waited for; matrix products, arithmetic and copies ran while one was open for 16% of the time, Pallas kernels for 21%

profile of v2, /device:TPU:0, one launch (start us, length us, event | category | flops | bytes accessed | tf_op | source)
XLA Modules:
  0.0 603.4 jit_solution(15469018912912485546)
XLA Ops:
  3.9 4.1 copy.203
  20.3 4.1 copy.207
  52.7 4.3 copy.213
  57.1 7.3 %all-to-all-start = ((bf16[1,256,8,6,1,128]{5,1,4,3,0,2:T(8,128)(2,1)}), bf16[1,256,8,6,1,128]{5,1,4,3,0,2:T(8,128)(2,1)S(1)}, u32[]{:S(2)}, u32[]{:S(2)}) async-start(bf16[1,256,8,6,1,128]{5,1,4,3,0,2:T(8,128)(2,1)} %copy.213), calls=%async_computation | async-start | bytes 6291456 | tf_op jit(solution)/shard_map/all_to_all | solution.py:172
  83.3 51.7 %all-to-all-done = bf16[1,256,8,6,1,128]{5,1,4,3,0,2:T(8,128)(2,1)S(1)} async-done(((bf16[1,256,8,6,1,128]{5,1,4,3,0,2:T(8,128)(2,1)}), bf16[1,256,8,6,1,128]{5,1,4,3,0,2:T(8,128)(2,1)S(1)}, u32[]{:S(2)}, u32[]{:S(2)}) %all-to-all-start) | async-done | bytes 3145760 | tf_op jit(solution)/shard_map/all_to_all | solution.py:172
  135.1 4.6 all-to-all-start.2
  158.7 51.2 %all-to-all-done.2 = bf16[1,256,8,6,1,128]{5,1,4,3,0,2:T(8,128)(2,1)} async-done(((bf16[1,256,8,6,1,128]{5,1,4,3,0,2:T(8,128)(2,1)}), bf16[1,256,8,6,1,128]{5,1,4,3,0,2:T(8,128)(2,1)}, u32[]{:S(2)}, u32[]{:S(2)}) %all-to-all-start.2) | async-done | bytes 3145760 | tf_op jit(solution)/shard_map/all_to_all | solution.py:172
  209.9 4.5 all-to-all-start.4
  233.4 51.1 %all-to-all-done.4 = bf16[1,256,8,6,1,128]{5,1,4,3,0,2:T(8,128)(2,1)} async-done(((bf16[1,256,8,6,1,128]{5,1,4,3,0,2:T(8,128)(2,1)}), bf16[1,256,8,6,1,128]{5,1,4,3,0,2:T(8,128)(2,1)}, u32[]{:S(2)}, u32[]{:S(2)}) %all-to-all-start.4) | async-done | bytes 3145760 | tf_op jit(solution)/shard_map/all_to_all | solution.py:172
  284.5 4.5 all-to-all-start.6
  295.8 31.4 %shard_map.104 = f32[2048,256]{1,0:T(8,128)} custom-call(s32[8]{0:T(128)} %get-tuple-element.10.first_ref, s32[8]{0:T(128)} %get-tuple-element.9.last_ref, s32[4]{0:T(128)} %bitcast.126, bf16[2048,768]{1,0:T(8,128)(2,1)} %bitcast.136, bf16[2048,768]{1,0:T(8,128)(2,1)} %bitcast.137, bf16[2048,768]{1,0:T(8,128)(2,1)} %bitcast.138, ...), custom_call_target="tpu_custom_call" | custom-call | tf_op jit(solution)/shard_map/pallas_call | solution.py:135
  330.4 28.7 %all-to-all-done.6 = bf16[1,256,8,6,1,128]{5,1,4,3,0,2:T(8,128)(2,1)} async-done(((bf16[1,256,8,6,1,128]{5,1,4,3,0,2:T(8,128)(2,1)}), bf16[1,256,8,6,1,128]{5,1,4,3,0,2:T(8,128)(2,1)}, u32[]{:S(2)}, u32[]{:S(2)}) %all-to-all-start.6) | async-done | bytes 3145760 | tf_op jit(solution)/shard_map/all_to_all | solution.py:172
  359.2 3.9 all-to-all-start.1
  363.0 4.1 copy.270
  369.5 31.4 %shard_map.105 = f32[2048,256]{1,0:T(8,128)} custom-call(s32[8]{0:T(128)} %get-tuple-element.10.first_ref, s32[8]{0:T(128)} %get-tuple-element.9.last_ref, s32[4]{0:T(128)} %bitcast.127, bf16[2048,768]{1,0:T(8,128)(2,1)} %bitcast.142, bf16[2048,768]{1,0:T(8,128)(2,1)} %bitcast.143, bf16[2048,768]{1,0:T(8,128)(2,1)} %bitcast.144, ...), custom_call_target="tpu_custom_call" | custom-call | tf_op jit(solution)/shard_map/pallas_call | solution.py:135
  400.9 3.3 reshape.165
  404.2 7.2 %all-to-all-done.1 = f32[1,2048,1,1,2,128]{5,4,3,2,0,1:T(2,128)S(1)} async-done(((f32[1,2048,1,1,2,128]{5,4,3,2,0,1:T(2,128)}), f32[1,2048,1,1,2,128]{5,4,3,2,0,1:T(2,128)S(1)}, u32[]{:S(2)}, u32[]{:S(2)}) %all-to-all-start.1) | async-done | bytes 2097184 | tf_op jit(solution)/shard_map/all_to_all | solution.py:175
  411.4 4.4 all-to-all-start.3
  415.8 4.1 copy.271
  422.3 31.4 %shard_map.106 = f32[2048,256]{1,0:T(8,128)} custom-call(s32[8]{0:T(128)} %get-tuple-element.10.first_ref, s32[8]{0:T(128)} %get-tuple-element.9.last_ref, s32[4]{0:T(128)} %bitcast.128, bf16[2048,768]{1,0:T(8,128)(2,1)} %bitcast.148, bf16[2048,768]{1,0:T(8,128)(2,1)} %bitcast.149, bf16[2048,768]{1,0:T(8,128)(2,1)} %bitcast.150, ...), custom_call_target="tpu_custom_call" | custom-call | tf_op jit(solution)/shard_map/pallas_call | solution.py:135
  456.9 6.7 %all-to-all-done.3 = f32[1,2048,1,1,2,128]{5,4,3,2,0,1:T(2,128)} async-done(((f32[1,2048,1,1,2,128]{5,4,3,2,0,1:T(2,128)}), f32[1,2048,1,1,2,128]{5,4,3,2,0,1:T(2,128)}, u32[]{:S(2)}, u32[]{:S(2)}) %all-to-all-start.3) | async-done | bytes 2097184 | tf_op jit(solution)/shard_map/all_to_all | solution.py:175
  463.6 4.6 all-to-all-start.5
  468.2 4.1 copy.272
  474.7 31.4 %shard_map.107 = f32[2048,256]{1,0:T(8,128)} custom-call(s32[8]{0:T(128)} %get-tuple-element.10.first_ref, s32[8]{0:T(128)} %get-tuple-element.9.last_ref, s32[4]{0:T(128)} %bitcast.129, bf16[2048,768]{1,0:T(8,128)(2,1)} %bitcast.130, bf16[2048,768]{1,0:T(8,128)(2,1)} %bitcast.131, bf16[2048,768]{1,0:T(8,128)(2,1)} %bitcast.132, ...), custom_call_target="tpu_custom_call" | custom-call | tf_op jit(solution)/shard_map/pallas_call | solution.py:135
  508.4 7.6 %all-to-all-done.5 = f32[1,2048,1,1,2,128]{5,4,3,2,0,1:T(2,128)} async-done(((f32[1,2048,1,1,2,128]{5,4,3,2,0,1:T(2,128)}), f32[1,2048,1,1,2,128]{5,4,3,2,0,1:T(2,128)}, u32[]{:S(2)}, u32[]{:S(2)}) %all-to-all-start.5) | async-done | bytes 2097184 | tf_op jit(solution)/shard_map/all_to_all | solution.py:175
  516.0 51.9 %all_to_all.132 = f32[1,2048,1,1,2,128]{5,4,3,2,0,1:T(2,128)S(1)} all-to-all(f32[1,2048,1,1,2,128]{5,4,3,2,0,1:T(2,128)S(1)} %bitcast.163), channel_id=1, replica_groups=mesh['groups'=2,'seq'=8,'samp'=2] {'seq'}, dimensions={1} | all-to-all | bytes 4194304 | tf_op jit(solution)/shard_map/all_to_all | solution.py:175
  567.9 5.1 pad_maximum_fusion
  573.0 7.5 %fusion.19 = (f32[1,256,8,4,1,128]{5,4,1,2,3,0:T(1,128)}, f32[1,256,8,4,1,128]{5,4,1,2,3,0:T(1,128)S(1)}) fusion(f32[1,256,8,4,2,128]{5,4,1,2,3,0:T(2,128)S(1)} %pad_maximum_fusion), kind=kLoop, calls=%fused_computation.86 | loop fusion | bytes 16777216 | tf_op jit(solution)/shard_map/slice | solution.py:182
  580.5 4.7 copy.267
  585.2 5.5 reshape_squeeze.6
  590.6 6.8 %copy.268 = f32[1,256,8,4,1,128]{5,3,2,1,4,0:T(4,128)} copy(f32[1,256,8,4,1,128]{5,4,1,2,3,0:T(1,128)} %get-tuple-element.11) | data formatting | bytes 8388608 | tf_op jit(solution)/shard_map/slice | solution.py:182
  597.5 5.5 reshape_squeeze.7
  (129 shorter events, 123.6 us)
Async XLA Ops:
  8.0 2.6 copy-start.1
  8.0 2.6 copy-start.18
  13.1 2.4 copy-start.3
  24.4 2.6 copy-start.2
  24.4 2.6 copy-start.19
  29.5 2.8 copy-start.4
  47.1 3.1 copy-start.7
  47.1 3.9 copy-start.8
  57.1 78.0 %all-to-all-start = ((bf16[1,256,8,6,1,128]{5,1,4,3,0,2:T(8,128)(2,1)}), bf16[1,256,8,6,1,128]{5,1,4,3,0,2:T(8,128)(2,1)S(1)}, u32[]{:S(2)}, u32[]{:S(2)}) async-start(bf16[1,256,8,6,1,128]{5,1,4,3,0,2:T(8,128)(2,1)} %copy.213), calls=%async_computation | async-start | bytes 6291456 | tf_op jit(solution)/shard_map/all_to_all | solution.py:172
  77.2 3.4 copy-start.16
  77.2 3.5 copy-start.14
  77.2 3.6 copy-start.9
  135.1 74.8 %all-to-all-start.2 = ((bf16[1,256,8,6,1,128]{5,1,4,3,0,2:T(8,128)(2,1)}), bf16[1,256,8,6,1,128]{5,1,4,3,0,2:T(8,128)(2,1)}, u32[]{:S(2)}, u32[]{:S(2)}) async-start(bf16[1,256,8,6,1,128]{5,1,4,3,0,2:T(8,128)(2,1)} %copy.228), calls=%async_computation.2 | async-start | bytes 6291456 | tf_op jit(solution)/shard_map/all_to_all | solution.py:172
  152.5 3.4 copy-start.17
  152.5 3.5 copy-start.15
  152.5 3.6 copy-start.10
  209.9 74.6 %all-to-all-start.4 = ((bf16[1,256,8,6,1,128]{5,1,4,3,0,2:T(8,128)(2,1)}), bf16[1,256,8,6,1,128]{5,1,4,3,0,2:T(8,128)(2,1)}, u32[]{:S(2)}, u32[]{:S(2)}) async-start(bf16[1,256,8,6,1,128]{5,1,4,3,0,2:T(8,128)(2,1)} %copy.243), calls=%async_computation.4 | async-start | bytes 6291456 | tf_op jit(solution)/shard_map/all_to_all | solution.py:172
  227.3 3.4 copy-start.11
  227.3 3.5 copy-start.12
  227.3 3.6 copy-start.13
  233.4 55.6 %copy-start.20 = (s32[2,4]{1,0:T(2,128)S(1)}, s32[2,4]{1,0:T(2,128)}, u32[]{:S(2)}) copy-start(s32[2,4]{1,0:T(2,128)} %param.19) | copy-start | bytes 100
  284.5 74.6 %all-to-all-start.6 = ((bf16[1,256,8,6,1,128]{5,1,4,3,0,2:T(8,128)(2,1)}), bf16[1,256,8,6,1,128]{5,1,4,3,0,2:T(8,128)(2,1)}, u32[]{:S(2)}, u32[]{:S(2)}) async-start(bf16[1,256,8,6,1,128]{5,1,4,3,0,2:T(8,128)(2,1)} %copy.258), calls=%async_computation.6 | async-start | bytes 6291456 | tf_op jit(solution)/shard_map/all_to_all | solution.py:172
  289.2 4.2 copy-start
  359.2 52.2 %all-to-all-start.1 = ((f32[1,2048,1,1,2,128]{5,4,3,2,0,1:T(2,128)}), f32[1,2048,1,1,2,128]{5,4,3,2,0,1:T(2,128)S(1)}, u32[]{:S(2)}, u32[]{:S(2)}) async-start(f32[1,2048,1,1,2,128]{5,4,3,2,0,1:T(2,128)} %bitcast.17), calls=%async_computation.1 | async-start | bytes 4194304 | tf_op jit(solution)/shard_map/all_to_all | solution.py:175
  411.4 8.4 %copy-start.5 = (f32[1,2048,1,1,2,128]{5,4,3,2,0,1:T(2,128)}, f32[1,2048,1,1,2,128]{5,4,3,2,0,1:T(2,128)S(1)}, u32[]{:S(2)}) copy-start(f32[1,2048,1,1,2,128]{5,4,3,2,0,1:T(2,128)S(1)} %all-to-all-done.1) | copy-start | bytes 6291460
  411.4 52.2 %all-to-all-start.3 = ((f32[1,2048,1,1,2,128]{5,4,3,2,0,1:T(2,128)}), f32[1,2048,1,1,2,128]{5,4,3,2,0,1:T(2,128)}, u32[]{:S(2)}, u32[]{:S(2)}) async-start(f32[1,2048,1,1,2,128]{5,4,3,2,0,1:T(2,128)} %bitcast.29), calls=%async_computation.3 | async-start | bytes 4194304 | tf_op jit(solution)/shard_map/all_to_all | solution.py:175
  463.6 52.4 %all-to-all-start.5 = ((f32[1,2048,1,1,2,128]{5,4,3,2,0,1:T(2,128)}), f32[1,2048,1,1,2,128]{5,4,3,2,0,1:T(2,128)}, u32[]{:S(2)}, u32[]{:S(2)}) async-start(f32[1,2048,1,1,2,128]{5,4,3,2,0,1:T(2,128)} %bitcast.41), calls=%async_computation.5 | async-start | bytes 4194304 | tf_op jit(solution)/shard_map/all_to_all | solution.py:175
  516.0 51.9 %copy-start.6 = (f32[1,2048,1,1,2,128]{5,4,3,2,0,1:T(2,128)S(1)}, f32[1,2048,1,1,2,128]{5,4,3,2,0,1:T(2,128)}, u32[]{:S(2)}) copy-start(f32[1,2048,1,1,2,128]{5,4,3,2,0,1:T(2,128)} %copy-done.5) | copy-start | bytes 6291460

commit v3 on v2

--- a/solution.py
+++ b/solution.py
@@ -10,6 +10,7 @@
 
 HEAD_DIM = 128
 BLOCK = 256
+KEY_BLOCK = 128
 
 
 def normalize(source, source_tangent, gain):
@@ -35,8 +36,9 @@
     last_segment = jnp.clip(last_segment, 0, samples - 1)
     first_key = jnp.take(sample_starts, first_segment)
     last_key = jnp.take(sample_ends, last_segment)
-    first_block = jnp.clip(first_key // BLOCK, 0, blocks - 1)
-    last_block = jnp.clip((last_key - 1) // BLOCK + 1, first_block + 1, blocks)
+    key_blocks = count // KEY_BLOCK
+    first_block = jnp.clip(first_key // KEY_BLOCK, 0, key_blocks - 1)
+    last_block = jnp.clip((last_key - 1) // KEY_BLOCK + 1, first_block + 1, key_blocks)
     return first_block.astype(jnp.int32), last_block.astype(jnp.int32), sample_ends
 
 
@@ -64,9 +66,9 @@
     last = last_ref[i]
 
     def scores_of(kb):
-        start = pl.multiple_of(kb * BLOCK, BLOCK)
-        key_rows = k_ref[pl.ds(start, BLOCK), :]
-        key_positions = start + lax.broadcasted_iota(jnp.int32, (1, BLOCK), 1)
+        start = pl.multiple_of(kb * KEY_BLOCK, KEY_BLOCK)
+        key_rows = k_ref[pl.ds(start, KEY_BLOCK), :]
+        key_positions = start + lax.broadcasted_iota(jnp.int32, (1, KEY_BLOCK), 1)
         same = query_segment == segment_of(key_positions)
         raw = lax.dot_general(
             queries, key_rows, (((1,), (1,)), ((), ())), preferred_element_type=jnp.float32
@@ -91,9 +93,9 @@
     def sums(kb, carry):
         center, output, spread_sum, dvalue_sum = carry
         raw, same, start, key_rows = scores_of(kb)
-        dkey_rows = dk_ref[pl.ds(start, BLOCK), :]
-        value_rows = v_ref[pl.ds(start, BLOCK), :]
-        dvalue_rows = dv_ref[pl.ds(start, BLOCK), :]
+        dkey_rows = dk_ref[pl.ds(start, KEY_BLOCK), :]
+        value_rows = v_ref[pl.ds(start, KEY_BLOCK), :]
+        dvalue_rows = dv_ref[pl.ds(start, KEY_BLOCK), :]
         both_keys = jnp.concatenate([key_rows, dkey_rows], axis=1)
         dscores = lax.dot_general(
             both_queries, both_keys, (((1,), (1,)), ((), ())), preferred_element_type=jnp.float32
@@ -112,8 +114,8 @@
     center, output, spread_sum, dvalue_sum = lax.fori_loop(
         first, last, sums, (jnp.zeros((BLOCK, 1), jnp.float32), empty, empty, empty)
     )
-    result_ref[:, :HEAD_DIM] = output.astype(result_ref.dtype)
-    result_ref[:, HEAD_DIM:] = (spread_sum - center * output + dvalue_sum).astype(result_ref.dtype)
+    result_ref[0] = output.astype(result_ref.dtype)
+    result_ref[1] = (spread_sum - center * output + dvalue_sum).astype(result_ref.dtype)
 
 
 def attend(stacked, heads, first_block, last_block, sample_ends, result_dtype):
@@ -130,12 +132,12 @@
         num_scalar_prefetch=3,
         grid=(heads, blocks),
         in_specs=[query_spec(0), query_spec(1), key_spec(2), key_spec(3), key_spec(4), key_spec(5)],
-        out_specs=pl.BlockSpec((BLOCK, 2 * HEAD_DIM), lambda h, i, *_: (i, h)),
+        out_specs=pl.BlockSpec((2, BLOCK, HEAD_DIM), lambda h, i, *_: (0, i, h)),
     )
     return pl.pallas_call(
         attention_kernel,
         grid_spec=grid_spec,
-        out_shape=jax.ShapeDtypeStruct((tokens, heads * 2 * HEAD_DIM), result_dtype),
+        out_shape=jax.ShapeDtypeStruct((2, tokens, heads * HEAD_DIM), result_dtype),
         compiler_params=pltpu.CompilerParams(
             dimension_semantics=("arbitrary", "arbitrary"),
         ),
@@ -143,7 +145,7 @@
 
 
 CHUNKS = 4
-RESULT_DTYPE = jnp.float32
+RESULT_DTYPE = jnp.bfloat16
 
 
 def per_device(
@@ -173,14 +175,13 @@
         stacked = moved.reshape(pack_tokens, 6 * chunk_heads * HEAD_DIM)
         result = attend(stacked, chunk_heads, first_block, last_block, sample_ends, RESULT_DTYPE)
         back = lax.all_to_all(
-            result.reshape(1, pack_tokens, 1, chunk_heads, 2, HEAD_DIM),
-            "seq", split_axis=1, concat_axis=2, tiled=True,
+            result.reshape(2, seq_count, tokens, chunk_heads * HEAD_DIM),
+            "seq", split_axis=1, concat_axis=1, tiled=True,
         )
         results.append(back)
-    joined = jnp.concatenate(results, axis=3).astype(jnp.float32)
-    output = joined[:, :, :, :, 0].reshape(1, tokens, width)
-    tangent = joined[:, :, :, :, 1].reshape(1, tokens, width)
-    return (output, tangent)
+    joined = jnp.concatenate(results, axis=3)
+    joined = jnp.swapaxes(joined, 1, 2).reshape(2, 1, tokens, width).astype(jnp.float32)
+    return (joined[0], joined[1])
 
 
 def solution(mesh):

time: 614 us -> 596 us (0.971); the launches traced: 603 us -> 594 us
  Pallas kernels: 125 us -> 187 us
  blocking collectives: 51.9 us -> 0 us
  waiting for transfers between devices: 204 us -> 192 us
  local copies, waits for them, and re-layouts: 170 us -> 159 us
  starting transfers between devices: 33.7 us -> 42.4 us
    pallas_call x4, Pallas kernels: 125 us -> 187 us  [attend(): pl.pallas_call(attention_kernel, grid_spec=grid_spec, out_shape=jax.Shape...]
    all_to_all x1 -> x0, blocking collectives: 51.9 us -> none  [per_device(): lax.all_to_all(result.reshape(1, pack_tokens, 1, chunk_heads, 2, HEAD_DIM...]
    slice x3 -> x1, local copies, waits for them, and re-layouts: 19 us -> 3.97 us  [per_device(): return (joined[0], joined[1])]
    all_to_all x4, waiting for transfers between devices: 183 us -> 168 us  [per_device(): lax.all_to_all(payload, 'seq', split_axis=2, concat_axis=1, tiled=True)]
    unnamed x72, local copies, waits for them, and re-layouts: 45.9 us -> 58.1 us
    another operation x3 -> x1, local copies, waits for them, and re-layouts: 10.9 us -> 0.01 us  [the longest x1 5.47 us: per_device(): output = joined[:, :, :, :, 0].reshape(1, tokens, width)]
    all_to_all x3 -> x4, starting transfers between devices: 12.8 us -> 21.6 us  [per_device(): lax.all_to_all(result.reshape(2, seq_count, tokens, chunk_heads * HEAD_DI...]
    all_to_all x3 -> x4, waiting for transfers between devices: 21.5 us -> 24.1 us  [per_device(): lax.all_to_all(result.reshape(2, seq_count, tokens, chunk_heads * HEAD_DI...]
  transfers between devices with their start and end apart: 7 -> 8, of which waited for: 7 -> 5; matrix products, arithmetic and copies ran while one was open for 16% -> 16% of each run, Pallas kernels for 21% -> 32%
where the time goes in v3:
time: 596 us; the launch traced here: 594 us
  waiting for transfers between devices  192 us (32%)
  Pallas kernels  187 us (31%)
  local copies, waits for them, and re-layouts  159 us (27%)
  starting transfers between devices  42.4 us (7%)
  other arithmetic  12.9 us (2%)
    pallas_call x4, Pallas kernels, attend(): pl.pallas_call(attention_kernel, grid_spec=grid_spec, out_shape=jax.Shape...  187 us
    all_to_all x4, waiting for transfers between devices, per_device(): lax.all_to_all(payload, 'seq', split_axis=2, concat_axis=1, tiled=True)  168 us
    unnamed x72, local copies, waits for them, and re-layouts  58.1 us
    slice x30, local copies, waits for them, and re-layouts, per_device(): payload = jnp.stack([array[:, :, :, heads] for array in split], axis=3)  54.1 us
    all_to_all x4, waiting for transfers between devices, per_device(): lax.all_to_all(result.reshape(2, seq_count, tokens, chunk_heads * HEAD_DI...  24.1 us
    all_to_all x4, starting transfers between devices, per_device(): lax.all_to_all(result.reshape(2, seq_count, tokens, chunk_heads * HEAD_DI...  21.6 us
    all_to_all x4, starting transfers between devices, per_device(): lax.all_to_all(payload, 'seq', split_axis=2, concat_axis=1, tiled=True)  20.8 us
    reshape x4, local copies, waits for them, and re-layouts, per_device(): stacked = moved.reshape(pack_tokens, 6 * chunk_heads * HEAD_DIM)  14.3 us
  transfers between devices with their start and end apart: 8, of which 5 were waited for; matrix products, arithmetic and copies ran while one was open for 16% of the time, Pallas kernels for 32%

profile of v3, /device:TPU:0, one launch (start us, length us, event | category | flops | bytes accessed | tf_op | source)
XLA Modules:
  0.0 594.4 jit_solution(16912458598316584587)
XLA Ops:
  0.6 3.3 copy.265
  3.9 4.1 copy.267
  8.0 2.6 fusion.10
  17.0 3.3 copy.269
  20.3 4.1 copy.271
  24.4 2.6 fusion.15
  35.7 3.3 copy.273
  42.5 3.3 copy.275
  52.7 4.3 copy.277
  57.0 7.3 %all-to-all-start = ((bf16[1,256,8,6,1,128]{5,1,4,3,0,2:T(8,128)(2,1)}), bf16[1,256,8,6,1,128]{5,1,4,3,0,2:T(8,128)(2,1)S(1)}, u32[]{:S(2)}, u32[]{:S(2)}) async-start(bf16[1,256,8,6,1,128]{5,1,4,3,0,2:T(8,128)(2,1)} %copy.277), calls=%async_computation | async-start | bytes 6291456 | tf_op jit(solution)/shard_map/all_to_all | solution.py:174
  83.3 51.7 %all-to-all-done = bf16[1,256,8,6,1,128]{5,1,4,3,0,2:T(8,128)(2,1)S(1)} async-done(((bf16[1,256,8,6,1,128]{5,1,4,3,0,2:T(8,128)(2,1)}), bf16[1,256,8,6,1,128]{5,1,4,3,0,2:T(8,128)(2,1)S(1)}, u32[]{:S(2)}, u32[]{:S(2)}) %all-to-all-start) | async-done | bytes 3145760 | tf_op jit(solution)/shard_map/all_to_all | solution.py:174
  135.0 4.6 all-to-all-start.2
  158.6 51.1 %all-to-all-done.2 = bf16[1,256,8,6,1,128]{5,1,4,3,0,2:T(8,128)(2,1)} async-done(((bf16[1,256,8,6,1,128]{5,1,4,3,0,2:T(8,128)(2,1)}), bf16[1,256,8,6,1,128]{5,1,4,3,0,2:T(8,128)(2,1)}, u32[]{:S(2)}, u32[]{:S(2)}) %all-to-all-start.2) | async-done | bytes 3145760 | tf_op jit(solution)/shard_map/all_to_all | solution.py:174
  209.8 4.4 all-to-all-start.4
  233.3 51.0 %all-to-all-done.4 = bf16[1,256,8,6,1,128]{5,1,4,3,0,2:T(8,128)(2,1)} async-done(((bf16[1,256,8,6,1,128]{5,1,4,3,0,2:T(8,128)(2,1)}), bf16[1,256,8,6,1,128]{5,1,4,3,0,2:T(8,128)(2,1)}, u32[]{:S(2)}, u32[]{:S(2)}) %all-to-all-start.4) | async-done | bytes 3145760 | tf_op jit(solution)/shard_map/all_to_all | solution.py:174
  284.3 4.5 all-to-all-start.6
  295.7 46.8 %shard_map.104 = bf16[2,2048,128]{2,1,0:T(8,128)(2,1)} custom-call(s32[8]{0:T(128)} %get-tuple-element.14.first_ref, s32[8]{0:T(128)} %get-tuple-element.13.last_ref, s32[4]{0:T(128)} %bitcast.106, bf16[2048,768]{1,0:T(8,128)(2,1)} %bitcast.116, bf16[2048,768]{1,0:T(8,128)(2,1)} %bitcast.117, bf16[2048,768]{1,0:T(8,128)(2,1)} %bitcast.118, ...), custom_call_target="tpu_custom_call" | custom-call | tf_op jit(solution)/shard_map/pallas_call | solution.py:137
  344.8 14.2 %all-to-all-done.6 = bf16[1,256,8,6,1,128]{5,1,4,3,0,2:T(8,128)(2,1)} async-done(((bf16[1,256,8,6,1,128]{5,1,4,3,0,2:T(8,128)(2,1)}), bf16[1,256,8,6,1,128]{5,1,4,3,0,2:T(8,128)(2,1)}, u32[]{:S(2)}, u32[]{:S(2)}) %all-to-all-start.6) | async-done | bytes 3145760 | tf_op jit(solution)/shard_map/all_to_all | solution.py:174
  359.0 3.8 all-to-all-start.1
  362.7 4.1 copy.338
  369.3 46.8 %shard_map.105 = bf16[2,2048,128]{2,1,0:T(8,128)(2,1)} custom-call(s32[8]{0:T(128)} %get-tuple-element.14.first_ref, s32[8]{0:T(128)} %get-tuple-element.13.last_ref, s32[4]{0:T(128)} %bitcast.107, bf16[2048,768]{1,0:T(8,128)(2,1)} %bitcast.122, bf16[2048,768]{1,0:T(8,128)(2,1)} %bitcast.123, bf16[2048,768]{1,0:T(8,128)(2,1)} %bitcast.124, ...), custom_call_target="tpu_custom_call" | custom-call | tf_op jit(solution)/shard_map/pallas_call | solution.py:137
  418.4 5.8 all-to-all-start.3
  424.2 4.1 copy.339
  430.7 46.8 %shard_map.106 = bf16[2,2048,128]{2,1,0:T(8,128)(2,1)} custom-call(s32[8]{0:T(128)} %get-tuple-element.14.first_ref, s32[8]{0:T(128)} %get-tuple-element.13.last_ref, s32[4]{0:T(128)} %bitcast.108, bf16[2048,768]{1,0:T(8,128)(2,1)} %bitcast.128, bf16[2048,768]{1,0:T(8,128)(2,1)} %bitcast.129, bf16[2048,768]{1,0:T(8,128)(2,1)} %bitcast.130, ...), custom_call_target="tpu_custom_call" | custom-call | tf_op jit(solution)/shard_map/pallas_call | solution.py:137
  479.8 6.0 %all-to-all-start.5 = ((bf16[2,8,256,128]{3,2,0,1:T(8,128)(2,1)}), bf16[2,8,256,128]{3,2,0,1:T(8,128)(2,1)S(1)}, u32[]{:S(2)}, u32[]{:S(2)}) async-start(bf16[2,8,256,128]{3,2,0,1:T(8,128)(2,1)} %copy.315), calls=%async_computation.5 | async-start | bytes 2097152 | tf_op jit(solution)/shard_map/all_to_all | solution.py:177
  485.8 4.1 copy.340
  492.4 46.8 %shard_map.107 = bf16[2,2048,128]{2,1,0:T(8,128)(2,1)} custom-call(s32[8]{0:T(128)} %get-tuple-element.14.first_ref, s32[8]{0:T(128)} %get-tuple-element.13.last_ref, s32[4]{0:T(128)} %bitcast.109, bf16[2048,768]{1,0:T(8,128)(2,1)} %bitcast.110, bf16[2048,768]{1,0:T(8,128)(2,1)} %bitcast.111, bf16[2048,768]{1,0:T(8,128)(2,1)} %bitcast.112, ...), custom_call_target="tpu_custom_call" | custom-call | tf_op jit(solution)/shard_map/pallas_call | solution.py:137
  542.4 6.0 %all-to-all-start.7 = ((bf16[2,8,256,128]{3,2,0,1:T(8,128)(2,1)}), bf16[2,8,256,128]{3,2,0,1:T(8,128)(2,1)}, u32[]{:S(2)}, u32[]{:S(2)}) async-start(bf16[2,8,256,128]{3,2,0,1:T(8,128)(2,1)} %copy.330), calls=%async_computation.7 | async-start | bytes 2097152 | tf_op jit(solution)/shard_map/all_to_all | solution.py:177
  551.0 24.1 %all-to-all-done.7 = bf16[2,8,256,128]{3,2,0,1:T(8,128)(2,1)} async-done(((bf16[2,8,256,128]{3,2,0,1:T(8,128)(2,1)}), bf16[2,8,256,128]{3,2,0,1:T(8,128)(2,1)}, u32[]{:S(2)}, u32[]{:S(2)}) %all-to-all-start.7) | async-done | bytes 1048608 | tf_op jit(solution)/shard_map/all_to_all | solution.py:177
  579.3 4.0 fusion.19
  583.2 5.6 copy.335
  588.8 5.6 copy.336
  (130 shorter events, 113.3 us)
Async XLA Ops:
  8.0 2.6 copy-start.1
  8.0 2.6 copy-start.17
  13.1 2.4 copy-start.3
  24.3 2.6 copy-start.2
  24.3 2.6 copy-start.18
  29.4 2.8 copy-start.4
  47.1 3.1 copy-start.6
  47.1 3.9 copy-start.7
  57.0 78.0 %all-to-all-start = ((bf16[1,256,8,6,1,128]{5,1,4,3,0,2:T(8,128)(2,1)}), bf16[1,256,8,6,1,128]{5,1,4,3,0,2:T(8,128)(2,1)S(1)}, u32[]{:S(2)}, u32[]{:S(2)}) async-start(bf16[1,256,8,6,1,128]{5,1,4,3,0,2:T(8,128)(2,1)} %copy.277), calls=%async_computation | async-start | bytes 6291456 | tf_op jit(solution)/shard_map/all_to_all | solution.py:174
  77.1 3.4 copy-start.15
  77.1 3.5 copy-start.13
  77.2 3.6 copy-start.8
  135.0 74.7 %all-to-all-start.2 = ((bf16[1,256,8,6,1,128]{5,1,4,3,0,2:T(8,128)(2,1)}), bf16[1,256,8,6,1,128]{5,1,4,3,0,2:T(8,128)(2,1)}, u32[]{:S(2)}, u32[]{:S(2)}) async-start(bf16[1,256,8,6,1,128]{5,1,4,3,0,2:T(8,128)(2,1)} %copy.292), calls=%async_computation.2 | async-start | bytes 6291456 | tf_op jit(solution)/shard_map/all_to_all | solution.py:174
  152.5 3.4 copy-start.16
  152.5 3.5 copy-start.14
  152.5 3.6 copy-start.9
  209.8 74.5 %all-to-all-start.4 = ((bf16[1,256,8,6,1,128]{5,1,4,3,0,2:T(8,128)(2,1)}), bf16[1,256,8,6,1,128]{5,1,4,3,0,2:T(8,128)(2,1)}, u32[]{:S(2)}, u32[]{:S(2)}) async-start(bf16[1,256,8,6,1,128]{5,1,4,3,0,2:T(8,128)(2,1)} %copy.307), calls=%async_computation.4 | async-start | bytes 6291456 | tf_op jit(solution)/shard_map/all_to_all | solution.py:174
  227.1 3.4 copy-start.10
  227.1 3.5 copy-start.11
  227.1 3.6 copy-start.12
  233.3 55.5 %copy-start.19 = (s32[2,4]{1,0:T(2,128)S(1)}, s32[2,4]{1,0:T(2,128)}, u32[]{:S(2)}) copy-start(s32[2,4]{1,0:T(2,128)} %param.19) | copy-start | bytes 100
  284.3 74.6 %all-to-all-start.6 = ((bf16[1,256,8,6,1,128]{5,1,4,3,0,2:T(8,128)(2,1)}), bf16[1,256,8,6,1,128]{5,1,4,3,0,2:T(8,128)(2,1)}, u32[]{:S(2)}, u32[]{:S(2)}) async-start(bf16[1,256,8,6,1,128]{5,1,4,3,0,2:T(8,128)(2,1)} %copy.322), calls=%async_computation.6 | async-start | bytes 6291456 | tf_op jit(solution)/shard_map/all_to_all | solution.py:174
  289.0 4.2 copy-start
  359.0 59.4 %all-to-all-start.1 = ((bf16[2,8,256,128]{3,2,0,1:T(8,128)(2,1)}), bf16[2,8,256,128]{3,2,0,1:T(8,128)(2,1)S(1)}, u32[]{:S(2)}, u32[]{:S(2)}) async-start(bf16[2,8,256,128]{3,2,0,1:T(8,128)(2,1)} %copy.285), calls=%async_computation.1 | async-start | bytes 2097152 | tf_op jit(solution)/shard_map/all_to_all | solution.py:177
  418.4 61.5 %all-to-all-start.3 = ((bf16[2,8,256,128]{3,2,0,1:T(8,128)(2,1)}), bf16[2,8,256,128]{3,2,0,1:T(8,128)(2,1)S(1)}, u32[]{:S(2)}, u32[]{:S(2)}) async-start(bf16[2,8,256,128]{3,2,0,1:T(8,128)(2,1)} %copy.300), calls=%async_computation.3 | async-start | bytes 2097152 | tf_op jit(solution)/shard_map/all_to_all | solution.py:177
  479.8 61.6 %all-to-all-start.5 = ((bf16[2,8,256,128]{3,2,0,1:T(8,128)(2,1)}), bf16[2,8,256,128]{3,2,0,1:T(8,128)(2,1)S(1)}, u32[]{:S(2)}, u32[]{:S(2)}) async-start(bf16[2,8,256,128]{3,2,0,1:T(8,128)(2,1)} %copy.315), calls=%async_computation.5 | async-start | bytes 2097152 | tf_op jit(solution)/shard_map/all_to_all | solution.py:177
  541.5 1.0 copy-start.5
  542.4 32.7 %all-to-all-start.7 = ((bf16[2,8,256,128]{3,2,0,1:T(8,128)(2,1)}), bf16[2,8,256,128]{3,2,0,1:T(8,128)(2,1)}, u32[]{:S(2)}, u32[]{:S(2)}) async-start(bf16[2,8,256,128]{3,2,0,1:T(8,128)(2,1)} %copy.330), calls=%async_computation.7 | async-start | bytes 2097152 | tf_op jit(solution)/shard_map/all_to_all | solution.py:177
